TPU v7x, 256 devices: a whole 4x4x8 slice. The times are simulated.
256 devices in a mesh: blk: 32 (over y, z), tp: 8 (over x, core).
Axes of the slice: x: 4, y: 4, z: 8, core: 2. Of those that a mesh axis runs over, the one named last changes fastest.
Arguments:
- queries: bfloat16 [32768, 1664], P(('blk', 'tp')), may hold values from -120 to 120
- keys: bfloat16 [32768, 1664], P(('blk', 'tp')), may hold values from -6 to 6
- values: bfloat16 [32768, 1664], P(('blk', 'tp')), may hold values from -6 to 6
- segment_ids: int32 [32768], replicated, may hold values from -1 to 31, as said below
- proj_weight: bfloat16 [6656, 3072], P(None, 'tp'), may hold values from -0.078125 to 0.078125
Outputs:
- normed: bfloat16 [8192, 3072], P('blk', 'tp')
- seg_peaks: float32 [32], replicated
Inputs may be any that keep to these rules, and one draw needn't show every extreme that they name: `segment_ids`: ids other than -1 never fall along the pack; every image 0 to 31 occurs as one run of tokens that starts at a multiple of 4 and has a multiple of 4 tokens, at most 1024; some image has exactly 1024; -1 marks padding tokens, which may stand between images.
All inputs are finite; a program needn't handle non-finite values.
Results may differ from a plain program's by a relative error of at most 0.0056.
Values may be sent and summed in bfloat16 or wider, within the bound.
No kernel may reach another device: no remote copies, remote signals or barrier semaphores. Data moves between devices by JAX's collectives and lax.ppermute only.
A program may use at most 128 MiB of HBM per device.

v0:
```python
import jax
import jax.numpy as jnp
from jax import lax
from jax.sharding import PartitionSpec as P

HEAD = 128
masked_score = -1e30
epsilon = 1e-06


def from_behind(x, axis, by):
    devices = lax.axis_size(axis)
    pairs = [(i, i + by) for i in range(devices) if 0 <= i + by < devices]
    return lax.ppermute(x, axis, pairs)


def key_scores(query_heads, key_heads):
    return jnp.einsum(
        "rhd,khd->hrk", query_heads, key_heads, preferred_element_type=jnp.float32
    ) * HEAD ** (-0.5)


def finish(scores, allowed, value_heads):
    scores = jnp.where(allowed[None], scores, masked_score)
    row_top = jnp.max(scores, axis=2, keepdims=True)
    exp_terms = jnp.where(allowed[None], jnp.exp(scores - row_top), 0.0)
    row_total = jnp.maximum(jnp.sum(exp_terms, axis=2), 1.0)
    weights = exp_terms.astype(jnp.bfloat16)
    mixed_out = jnp.einsum("hrk,khd->rhd", weights, value_heads, preferred_element_type=jnp.float32)
    return mixed_out / row_total.T[:, :, None]


def per_device(queries, keys, values, segment_ids, proj_weight):
    group_count = lax.axis_size("blk")
    group_index = lax.axis_index("blk")
    part_index = lax.axis_index("tp")
    row_count = queries.shape[0]
    width = queries.shape[1]
    heads_count = width // HEAD
    block_len = segment_ids.shape[0] // group_count
    own_begin = group_index * block_len
    query_segs = lax.dynamic_slice_in_dim(
        segment_ids, own_begin + part_index * row_count, row_count
    )
    own_keys, own_values = (
        lax.all_gather(keys, "tp", axis=0, tiled=True),
        lax.all_gather(values, "tp", axis=0, tiled=True),
    )
    before_keys, before_values = from_behind((own_keys, own_values), "blk", 1)
    after_keys, after_values = from_behind((own_keys, own_values), "blk", -1)

    def neighbor_segs(offset):
        target = group_index + offset
        inside = (target >= 0) & (target < group_count)
        begin_at = jnp.clip(target, 0, group_count - 1) * block_len
        return jnp.where(inside, lax.dynamic_slice_in_dim(segment_ids, begin_at, block_len), -2)

    seg_sets = (neighbor_segs(-1), neighbor_segs(0), neighbor_segs(1))
    key_sets = (before_keys, own_keys, after_keys)
    masks = [
        (query_segs[:, None] == key_segs[None, :]) & (query_segs[:, None] >= 0)
        for key_segs in seg_sets
    ]
    query_heads = queries.reshape(row_count, heads_count, HEAD)
    all_keys = jnp.concatenate(key_sets, axis=0).reshape(3 * block_len, heads_count, HEAD)
    scores = key_scores(query_heads, all_keys)
    full_mask = jnp.concatenate(masks, axis=1)
    value_heads = jnp.concatenate((before_values, own_values, after_values), axis=0).reshape(
        3 * block_len, heads_count, HEAD
    )
    attended = finish(scores, full_mask, value_heads).reshape(row_count, width).astype(jnp.bfloat16)
    merged = attended.reshape(row_count // 4, 4 * width)
    projected = jnp.dot(
        lax.all_gather(merged, "tp", axis=0, tiled=True),
        proj_weight,
        preferred_element_type=jnp.float32,
    )
    row_segs = lax.dynamic_slice_in_dim(segment_ids, own_begin, block_len)[::4]
    member = row_segs[:, None] == jnp.arange(group_count, dtype=jnp.int32)[None, :]
    squares = jnp.sum(projected * projected, axis=1)
    seg_sums = jnp.sum(jnp.where(member, squares[:, None], 0.0), axis=0)
    seg_counts = jnp.sum(member.astype(jnp.float32), axis=0) * projected.shape[1]
    row_peak = jnp.max(jnp.where(member, jnp.max(projected, axis=1)[:, None], masked_score), axis=0)
    seg_sums, seg_counts = lax.psum((seg_sums, seg_counts), ("blk", "tp"))
    row_peak = lax.pmax(row_peak, ("blk", "tp"))
    seg_scale = lax.rsqrt(seg_sums / seg_counts + epsilon)
    row_scale = jnp.sum(jnp.where(member, seg_scale[None, :], 0.0), axis=1)
    normed = (projected * row_scale[:, None]).astype(jnp.bfloat16)
    return (normed, row_peak * seg_scale)


def solution(mesh):
    in_specs = (
        P(("blk", "tp"), None),
        P(("blk", "tp"), None),
        P(("blk", "tp"), None),
        P(),
        P(None, "tp"),
    )
    out_specs = (P("blk", "tp"), P())
    return jax.shard_map(
        per_device, mesh=mesh, in_specs=in_specs, out_specs=out_specs, check_vma=False
    )
```

profile of v0, /device:TPU:1, one launch (start us, length us, event | category | flops | bytes accessed | tf_op | source)
XLA Modules:
  0.0 441.4 jit_solution(14741535118343284138)
XLA Ops:
  7.2 2.0 copy.18
  9.3 0.7 all-gather.4.cloned.1.call-update
  10.0 39.3 %all-gather.6.cloned.1.call-done = bf16[1024,1664]{0,1:T(8,128)(2,1)} async-done(((bf16[128,1664]{0,1:T(8,128)(2,1)}), bf16[1024,1664]{0,1:T(8,128)(2,1)}) %all-gather.6.cloned.1.call-update) | async-done | bytes 3407888 | tf_op jit(solution)/shard_map/all_gather | solution.py:46
  49.4 1.3 collective-permute-start.3
  50.6 5.8 %collective-permute-start.2 = (bf16[1024,1664]{0,1:T(8,128)(2,1)}, bf16[1024,1664]{0,1:T(8,128)(2,1)}, u32[]{:S(2)}, u32[]{:S(2)}) collective-permute-start(bf16[1024,1664]{0,1:T(8,128)(2,1)} %all-gather.6.cloned.1.call-done), channel_id=1, source_target_pairs={{0,8},{8,16},{16,24},{24,32},{32,40},{40,48},{48,56},{56,64},{64,7... | collective-permute-start | bytes 10223624 | tf_op jit(solution)/shard_map/ppermute | solution.py:14
  56.4 2.0 copy.19
  58.4 0.8 broadcast_compare_fusion
  59.1 0.8 fusion.21
  60.0 23.7 %all-gather.4.cloned.1.call-done = bf16[1024,1664]{1,0:T(8,128)(2,1)} async-done(((bf16[128,1664]{1,0:T(8,128)(2,1)}), bf16[1024,1664]{1,0:T(8,128)(2,1)}) %all-gather.4.cloned.1.call-update) | async-done | bytes 3407888 | tf_op jit(solution)/shard_map/all_gather | solution.py:47
  83.6 1.3 collective-permute-start.1
  84.9 5.9 %collective-permute-start = (bf16[1024,1664]{1,0:T(8,128)(2,1)}, bf16[1024,1664]{1,0:T(8,128)(2,1)}, u32[]{:S(2)}, u32[]{:S(2)}) collective-permute-start(bf16[1024,1664]{1,0:T(8,128)(2,1)} %all-gather.4.cloned.1.call-done), channel_id=1, source_target_pairs={{0,8},{8,16},{16,24},{24,32},{32,40},{40,48},{48,56},{56,64},{64,7... | collective-permute-start | bytes 10223624 | tf_op jit(solution)/shard_map/ppermute | solution.py:14
  90.8 0.7 compare_and_fusion.2
  91.5 0.8 pad_add_fusion
  92.2 34.3 %collective-permute-done.3 = bf16[1024,1664]{0,1:T(8,128)(2,1)S(1)} collective-permute-done((bf16[1024,1664]{0,1:T(8,128)(2,1)}, bf16[1024,1664]{0,1:T(8,128)(2,1)S(1)}, u32[]{:S(2)}, u32[]{:S(2)}) %collective-permute-start.3) | collective-permute-done | bytes 3407904 | tf_op jit(solution)/shard_map/ppermute | solution.py:14
  126.5 1.0 collective-permute-done.2
  127.5 7.9 %pad_maximum_fusion.1 = bf16[3072,1664]{0,1:T(8,128)(2,1)} fusion(bf16[1024,1664]{0,1:T(8,128)(2,1)S(1)} %collective-permute-done.3, bf16[1024,1664]{0,1:T(8,128)(2,1)} %all-gather.6.cloned.1.call-done, bf16[1024,1664]{0,1:T(8,128)(2,1)} %collective-permute-done.2), kind=kLoop, calls=%fused_computation.5 | loop fusion | flops 30670848 | bytes 20447232 | tf_op jit(solution)/shard_map/concatenate | solution.py:65
  135.4 17.8 %fusion.22 = (f32[13,128]{1,0:T(8,128)S(1)}, bf16[13,128,3072]{1,2,0:T(8,128)(2,1)}) fusion(pred[128,3072]{0,1:T(8,128)(4,1)} %pad_add_fusion, bf16[3072,13,128]{0,2,1:T(8,128)(2,1)} %bitcast.30, bf16[128,13,128]{0,2,1:T(8,128)(2,1)} %bitcast.32), kind=kOutput, calls=%fused_computation.37 | convolution fusion | flops 1339296768 | bytes 21273088 | tf_op jit(solution)/shard_map/sub | solution.py:26
  153.2 46.5 %collective-permute-done.1 = bf16[1024,1664]{1,0:T(8,128)(2,1)} collective-permute-done((bf16[1024,1664]{1,0:T(8,128)(2,1)}, bf16[1024,1664]{1,0:T(8,128)(2,1)}, u32[]{:S(2)}, u32[]{:S(2)}) %collective-permute-start.1) | collective-permute-done | bytes 3407904 | tf_op jit(solution)/shard_map/ppermute | solution.py:14
  199.7 0.9 collective-permute-done
  200.5 15.7 %pad_maximum_fusion = bf16[3072,1664]{1,0:T(8,128)(2,1)} fusion(bf16[1024,1664]{1,0:T(8,128)(2,1)} %collective-permute-done.1, bf16[1024,1664]{1,0:T(8,128)(2,1)S(1)} %copy-done, bf16[1024,1664]{1,0:T(8,128)(2,1)} %collective-permute-done), kind=kLoop, calls=%fused_computation.4 | loop fusion | flops 30670848 | bytes 20447232 | tf_op jit(solution)/shard_map/concatenate | solution.py:68
  216.2 14.3 %copy.17 = bf16[3072,1664]{0,1:T(8,128)(2,1)} copy(bf16[3072,1664]{1,0:T(8,128)(2,1)} %pad_maximum_fusion) | data formatting | bytes 20447232 | tf_op jit(solution)/shard_map/concatenate | solution.py:68
  230.6 9.6 %fusion.15 = bf16[128,13,128]{0,2,1:T(8,128)(2,1)S(1)} fusion(bf16[3072,13,128]{0,2,1:T(8,128)(2,1)} %bitcast.31, bf16[13,128,3072]{1,2,0:T(8,128)(2,1)} %get-tuple-element.20, f32[128,13]{0,1:T(8,128)S(1)} %maximum_bitcast_fusion), kind=kOutput, calls=%fused_computation.15 | convolution fusion | flops 1309048832 | bytes 20879872 | tf_op jit(solution)/shard_map/hrk,khd->rhd/dot_general | solution.py:29
  240.2 0.4 copy.23
  240.6 1.1 convert_element_type.18
  241.7 0.2 slice.3
  241.9 35.6 %all-gather.8.cloned.1.call-done = bf16[256,6656]{1,0:T(8,128)(2,1)} async-done(((bf16[32,6656]{1,0:T(8,128)(2,1)}), bf16[256,6656]{1,0:T(8,128)(2,1)}) %all-gather.8.cloned.1.call-update) | async-done | bytes 3407888 | tf_op jit(solution)/shard_map/all_gather | solution.py:74
  277.5 5.5 %fusion.20 = (f32[256]{0:T(256)S(1)}, f32[256]{0:T(256)S(1)}, f32[256,384]{1,0:T(8,128)S(1)}) fusion(bf16[256,6656]{1,0:T(8,128)(2,1)} %all-gather.8.cloned.1.call-done, bf16[6656,384]{1,0:T(8,128)(2,1)} %param.9), kind=kOutput, calls=%fused_computation.35 | convolution fusion | flops 1308917248 | bytes 8914944 | tf_op jit(solution)/shard_map/dot_general | solution.py:73
  283.2 76.2 %all-reduce = (f32[32]{0:T(128)S(1)}, f32[32]{0:T(128)S(1)}) all-reduce(f32[32]{0:T(128)S(1)} %get-tuple-element.7, f32[32]{0:T(128)S(1)} %broadcast_multiply_fusion), channel_id=1, replica_groups=mesh['blk'=32,'tp'=8] {'blk','tp'}, use_global_device_ids=true, to_apply=%region_4.5 | all-reduce | flops 64 | bytes 512 | tf_op jit(solution)/shard_map/psum | solution.py:84
  359.5 0.1 select_reduce_fusion
  359.6 74.0 %pmax.7 = f32[32]{0:T(128)S(1)} all-reduce(f32[32]{0:T(128)S(1)} %get-tuple-element.4), channel_id=1, replica_groups=mesh['blk'=32,'tp'=8] {'blk','tp'}, use_global_device_ids=true, to_apply=%region_10.11 | all-reduce | flops 32 | bytes 256 | tf_op jit(solution)/shard_map/pmax | solution.py:85
  433.6 0.5 mul.57
  434.1 0.8 multiply_convert_fusion
  (11 shorter events, 0.3 us)
Async XLA Ops:
  7.2 42.2 %all-gather.6.cloned.1.call-start = ((), (), s32[]{:S(2)}) async-start(), calls=%async_computation.1 | async-start | bytes 3833856 | tf_op jit(solution)/shard_map/all_gather | solution.py:46
  9.2 74.4 %all-gather.4.cloned.1.call-start = ((), (), s32[]{:S(2)}) async-start(), calls=%async_computation | async-start | bytes 3833856 | tf_op jit(solution)/shard_map/all_gather | solution.py:47
  10.0 267.6 %all-gather.8.cloned.1.call-start = ((), (), s32[]{:S(2)}) async-start(), calls=%async_computation.2 | async-start | bytes 3833856 | tf_op jit(solution)/shard_map/all_gather | solution.py:74
  49.4 77.2 %collective-permute-start.3 = (bf16[1024,1664]{0,1:T(8,128)(2,1)}, bf16[1024,1664]{0,1:T(8,128)(2,1)S(1)}, u32[]{:S(2)}, u32[]{:S(2)}) collective-permute-start(bf16[1024,1664]{0,1:T(8,128)(2,1)} %all-gather.6.cloned.1.call-done), channel_id=1, source_target_pairs={{8,0},{16,8},{24,16},{32,24},{40,32},{48,40},{56,48},{64,56},{72,6... | collective-permute-start | bytes 10223624 | tf_op jit(solution)/shard_map/ppermute | solution.py:14
  50.6 76.8 %collective-permute-start.2 = (bf16[1024,1664]{0,1:T(8,128)(2,1)}, bf16[1024,1664]{0,1:T(8,128)(2,1)}, u32[]{:S(2)}, u32[]{:S(2)}) collective-permute-start(bf16[1024,1664]{0,1:T(8,128)(2,1)} %all-gather.6.cloned.1.call-done), channel_id=1, source_target_pairs={{0,8},{8,16},{16,24},{24,32},{32,40},{40,48},{48,56},{56,64},{64,7... | collective-permute-start | bytes 10223624 | tf_op jit(solution)/shard_map/ppermute | solution.py:14
  83.6 116.0 %collective-permute-start.1 = (bf16[1024,1664]{1,0:T(8,128)(2,1)}, bf16[1024,1664]{1,0:T(8,128)(2,1)}, u32[]{:S(2)}, u32[]{:S(2)}) collective-permute-start(bf16[1024,1664]{1,0:T(8,128)(2,1)} %all-gather.4.cloned.1.call-done), channel_id=1, source_target_pairs={{8,0},{16,8},{24,16},{32,24},{40,32},{48,40},{56,48},{64,56},{72,6... | collective-permute-start | bytes 10223624 | tf_op jit(solution)/shard_map/ppermute | solution.py:14
  84.9 115.6 %collective-permute-start = (bf16[1024,1664]{1,0:T(8,128)(2,1)}, bf16[1024,1664]{1,0:T(8,128)(2,1)}, u32[]{:S(2)}, u32[]{:S(2)}) collective-permute-start(bf16[1024,1664]{1,0:T(8,128)(2,1)} %all-gather.4.cloned.1.call-done), channel_id=1, source_target_pairs={{0,8},{8,16},{16,24},{24,32},{32,40},{40,48},{48,56},{56,64},{64,7... | collective-permute-start | bytes 10223624 | tf_op jit(solution)/shard_map/ppermute | solution.py:14
  135.4 65.1 %copy-start = (bf16[1024,1664]{1,0:T(8,128)(2,1)S(1)}, bf16[1024,1664]{1,0:T(8,128)(2,1)}, u32[]{:S(2)}) copy-start(bf16[1024,1664]{1,0:T(8,128)(2,1)} %all-gather.4.cloned.1.call-done) | copy-start | bytes 10223620
Sparse Core Ops, SparseCore 0:
  9.8 39.4 all-gather.5
  51.2 32.3 all-gather.3
  241.9 35.6 all-gather.7
where the time goes:
time: 442 us; the launch traced here: 441 us
  waiting for transfers between devices  182 us (41%)
  blocking collectives  150 us (34%)
  matrix products  32.9 us (7%)
  other arithmetic  28.2 us (6%)
  local copies, waits for them, and re-layouts  20 us (5%)
  starting transfers between devices  14.3 us (3%)
  between operations  13.8 us (3%)
    ppermute x4, waiting for transfers between devices, from_behind(): return lax.ppermute(x, axis, pairs)  82.6 us
    psum x1, blocking collectives, per_device(): seg_sums, seg_counts = lax.psum((seg_sums, seg_counts), ('blk', 'tp'))  76.2 us
    pmax x1, blocking collectives, per_device(): row_peak = lax.pmax(row_peak, ('blk', 'tp'))  74 us
    all_gather x1, waiting for transfers between devices, per_device(): lax.all_gather(keys, 'tp', axis=0, tiled=True)  39.3 us
    all_gather x1, waiting for transfers between devices, per_device(): lax.all_gather(merged, 'tp', axis=0, tiled=True)  35.6 us
    all_gather x1, waiting for transfers between devices, per_device(): lax.all_gather(values, 'tp', axis=0, tiled=True)  23.7 us
    sub x1, matrix products, finish(): exp_terms = jnp.where(allowed[None], jnp.exp(scores - row_top), 0.0)  17.8 us
    concatenate x1, other arithmetic, per_device(): jnp.concatenate((before_values, own_values, after_values), axis=0)  15.7 us
  transfers between devices with their start and end apart: 7, of which 7 were waited for; matrix products, arithmetic and copies ran while one was open for 7% of the time, Pallas kernels for 0%

commit v1 on v0

--- a/solution.py
+++ b/solution.py
@@ -1,11 +1,26 @@
+import functools
 import jax
 import jax.numpy as jnp
 from jax import lax
 from jax.sharding import PartitionSpec as P
+from jax.lax import all_to_all, axis_size
 
 HEAD = 128
 masked_score = -1e30
 epsilon = 1e-06
+
+
+def convert_the_plane(buf, net_axis):
+    low = jnp.concatenate(
+        all_to_all(
+            jnp.stack(axis_size(net_axis) * [buf]), axis_name=net_axis, split_axis=0, concat_axis=0
+        ),
+        0,
+    )
+    return low
+
+
+watch_the_rings = functools.partial(convert_the_plane, net_axis="tp")
 
 
 def from_behind(x, axis, by):
@@ -42,10 +57,7 @@
     query_segs = lax.dynamic_slice_in_dim(
         segment_ids, own_begin + part_index * row_count, row_count
     )
-    own_keys, own_values = (
-        lax.all_gather(keys, "tp", axis=0, tiled=True),
-        lax.all_gather(values, "tp", axis=0, tiled=True),
-    )
+    own_keys, own_values = (lax.all_gather(keys, "tp", axis=0, tiled=True), watch_the_rings(values))
     before_keys, before_values = from_behind((own_keys, own_values), "blk", 1)
     after_keys, after_values = from_behind((own_keys, own_values), "blk", -1)
 

time: 442 us -> 465 us (1.052)
  blocking collectives: 150 us -> 210 us
  waiting for transfers between devices: 182 us -> 139 us
  local copies, waits for them, and re-layouts: 20 us -> 41.1 us
  other arithmetic: 28.2 us -> 12.5 us
    all_to_all x0 -> x1, blocking collectives: none -> 59.9 us  [convert_the_plane(): all_to_all(jnp.stack(axis_size(net_axis) * [buf]), axis_name=net_axis, sp...]
    all_gather x1, waiting for transfers between devices: 39.3 us -> 0.02 us  [per_device(): lax.all_gather(keys, 'tp', axis=0, tiled=True)]
    ppermute x4, waiting for transfers between devices: 82.6 us -> 107 us  [from_behind(): return lax.ppermute(x, axis, pairs)]
    all_gather x1 -> x0, waiting for transfers between devices: 23.7 us -> none  [per_device(): lax.all_gather(values, 'tp', axis=0, tiled=True)]
    concatenate x1 -> x0, other arithmetic: 15.7 us -> none  [per_device(): jnp.concatenate((before_values, own_values, after_values), axis=0)]
    all_to_all x0 -> x2, local copies, waits for them, and re-layouts: none -> 15 us  [convert_the_plane(): all_to_all(jnp.stack(axis_size(net_axis) * [buf]), axis_name=net_axis, sp...]
    ppermute x0 -> x2, local copies, waits for them, and re-layouts: none -> 11.1 us  [from_behind(): return lax.ppermute(x, axis, pairs)]
    concatenate x1, local copies, waits for them, and re-layouts: 14.3 us -> 6.61 us  [per_device(): jnp.concatenate((before_values, own_values, after_values), axis=0)]
  transfers between devices with their start and end apart: 7 -> 6, of which waited for: 7 -> 4; matrix products, arithmetic and copies ran while one was open for 7% -> 9% of each run, Pallas kernels for 0% -> 0%
where the time goes in v1:
time: 465 us; the launch traced here: 464 us
  blocking collectives  210 us (45%)
  waiting for transfers between devices  139 us (30%)
  local copies, waits for them, and re-layouts  41.1 us (9%)
  matrix products  32.9 us (7%)
  between operations  14.1 us (3%)
  starting transfers between devices  13.6 us (3%)
  other arithmetic  12.5 us (3%)
    ppermute x4, waiting for transfers between devices, from_behind(): return lax.ppermute(x, axis, pairs)  107 us
    psum x1, blocking collectives, per_device(): seg_sums, seg_counts = lax.psum((seg_sums, seg_counts), ('blk', 'tp'))  76.2 us
    pmax x1, blocking collectives, per_device(): row_peak = lax.pmax(row_peak, ('blk', 'tp'))  74 us
    all_to_all x1, blocking collectives, convert_the_plane(): all_to_all(jnp.stack(axis_size(net_axis) * [buf]), axis_name=net_axis, sp...  59.9 us
    all_gather x1, waiting for transfers between devices, per_device(): lax.all_gather(merged, 'tp', axis=0, tiled=True)  32.2 us
    sub x1, matrix products, finish(): exp_terms = jnp.where(allowed[None], jnp.exp(scores - row_top), 0.0)  17.9 us
    all_to_all x2, local copies, waits for them, and re-layouts, convert_the_plane(): all_to_all(jnp.stack(axis_size(net_axis) * [buf]), axis_name=net_axis, sp...  15 us
    ppermute x4, starting transfers between devices, from_behind(): return lax.ppermute(x, axis, pairs)  13.5 us
  transfers between devices with their start and end apart: 6, of which 4 were waited for; matrix products, arithmetic and copies ran while one was open for 9% of the time, Pallas kernels for 0%

profile of v1, /device:TPU:1, one launch (start us, length us, event | category | flops | bytes accessed | tf_op | source)
XLA Modules:
  0.0 463.6 jit_solution(8590219905536601422)
XLA Ops:
  7.2 2.0 copy.41
  9.3 1.3 copy.36
  10.5 0.4 stack.2
  11.0 59.9 %all_to_all.5 = bf16[8,128,1664]{1,2,0:T(8,128)(2,1)S(1)} all-to-all(bf16[8,128,1664]{1,2,0:T(8,128)(2,1)S(1)} %stack.2), channel_id=1, replica_groups=mesh['blk'=32,'tp'=8] {'tp'}, dimensions={0} | all-to-all | bytes 6815744 | tf_op jit(solution)/shard_map/all_to_all | solution.py:15
  70.8 4.1 copy.37
  74.9 5.2 %collective-permute-start = (bf16[1024,1664]{1,0:T(8,128)(2,1)}, bf16[1024,1664]{1,0:T(8,128)(2,1)}, u32[]{:S(2)}, u32[]{:S(2)}) collective-permute-start(bf16[1024,1664]{1,0:T(8,128)(2,1)} %bitcast.32), channel_id=1, source_target_pairs={{0,8},{8,16},{16,24},{24,32},{32,40},{40,48},{48,56},{56,64},{64,7... | collective-permute-start | bytes 10223624 | tf_op jit(solution)/shard_map/ppermute | solution.py:29
  80.1 1.3 collective-permute-start.1
  81.4 5.8 %collective-permute-start.2 = (bf16[1024,1664]{0,1:T(8,128)(2,1)}, bf16[1024,1664]{0,1:T(8,128)(2,1)}, u32[]{:S(2)}, u32[]{:S(2)}) collective-permute-start(bf16[1024,1664]{0,1:T(8,128)(2,1)} %all-gather.3.cloned.1.call-done), channel_id=1, source_target_pairs={{0,8},{8,16},{16,24},{24,32},{32,40},{40,48},{48,56},{56,64},{64,7... | collective-permute-start | bytes 10223624 | tf_op jit(solution)/shard_map/ppermute | solution.py:29
  87.2 1.3 collective-permute-start.3
  88.5 2.0 copy.42
  90.5 0.8 broadcast_compare_fusion
  91.3 0.8 fusion.27
  92.1 0.7 compare_and_fusion.2
  92.8 0.8 pad_add_fusion
  93.6 10.9 %copy.39 = bf16[8,128,1664]{1,0,2:T(8,128)(2,1)} copy(bf16[8,128,1664]{1,2,0:T(8,128)(2,1)S(1)} %all_to_all.5) | data formatting | bytes 6815744 | tf_op jit(solution)/shard_map/all_to_all | solution.py:15
  104.5 6.6 %concatenate.17 = bf16[1024,13,128]{0,2,1:T(8,128)(2,1)} reshape(bf16[8,128,1664]{1,0,2:T(8,128)(2,1)} %copy.39) | data formatting | bytes 6815744 | tf_op jit(solution)/shard_map/concatenate | solution.py:80
  111.1 39.6 %collective-permute-done = bf16[1024,1664]{1,0:T(8,128)(2,1)} collective-permute-done((bf16[1024,1664]{1,0:T(8,128)(2,1)}, bf16[1024,1664]{1,0:T(8,128)(2,1)}, u32[]{:S(2)}, u32[]{:S(2)}) %collective-permute-start) | collective-permute-done | bytes 3407904 | tf_op jit(solution)/shard_map/ppermute | solution.py:29
  150.7 5.6 %copy.38 = bf16[1024,1664]{0,1:T(8,128)(2,1)} copy(bf16[1024,1664]{1,0:T(8,128)(2,1)} %collective-permute-done) | data formatting | bytes 6815744 | tf_op jit(solution)/shard_map/ppermute | solution.py:29
  156.2 5.6 %copy.40 = bf16[1024,1664]{0,1:T(8,128)(2,1)} copy(bf16[1024,1664]{1,0:T(8,128)(2,1)} %collective-permute-done.1) | data formatting | bytes 6815744 | tf_op jit(solution)/shard_map/ppermute | solution.py:29
  161.8 61.9 %collective-permute-done.2 = bf16[1024,1664]{0,1:T(8,128)(2,1)} collective-permute-done((bf16[1024,1664]{0,1:T(8,128)(2,1)}, bf16[1024,1664]{0,1:T(8,128)(2,1)}, u32[]{:S(2)}, u32[]{:S(2)}) %collective-permute-start.2) | collective-permute-done | bytes 3407904 | tf_op jit(solution)/shard_map/ppermute | solution.py:29
  223.7 5.5 %collective-permute-done.3 = bf16[1024,1664]{0,1:T(8,128)(2,1)} collective-permute-done((bf16[1024,1664]{0,1:T(8,128)(2,1)}, bf16[1024,1664]{0,1:T(8,128)(2,1)}, u32[]{:S(2)}, u32[]{:S(2)}) %collective-permute-start.3) | collective-permute-done | bytes 3407904 | tf_op jit(solution)/shard_map/ppermute | solution.py:29
  229.2 7.9 %pad_maximum_fusion = bf16[3072,1664]{0,1:T(8,128)(2,1)} fusion(bf16[1024,1664]{0,1:T(8,128)(2,1)} %collective-permute-done.3, bf16[1024,1664]{0,1:T(8,128)(2,1)S(1)} %copy-done, bf16[1024,1664]{0,1:T(8,128)(2,1)} %collective-permute-done.2), kind=kLoop, calls=%fused_computation.10 | loop fusion | flops 30670848 | bytes 20447232 | tf_op jit(solution)/shard_map/concatenate | solution.py:77
  237.2 17.9 %fusion.28 = (f32[13,128]{1,0:T(8,128)S(1)}, bf16[13,128,3072]{1,2,0:T(8,128)(2,1)}) fusion(pred[128,3072]{0,1:T(8,128)(4,1)} %pad_add_fusion, bf16[3072,13,128]{0,2,1:T(8,128)(2,1)} %bitcast.31, bf16[128,13,128]{0,2,1:T(8,128)(2,1)} %bitcast.36), kind=kOutput, calls=%fused_computation.41 | convolution fusion | flops 1339296768 | bytes 21273088 | tf_op jit(solution)/shard_map/sub | solution.py:41
  255.1 9.5 %divide_convert_fusion = bf16[128,13,128]{0,2,1:T(8,128)(2,1)} fusion(bf16[13,128,3072]{1,2,0:T(8,128)(2,1)} %get-tuple-element.20, bf16[1024,13,128]{0,2,1:T(8,128)(2,1)} %bitcast.35, bf16[1024,13,128]{0,2,1:T(8,128)(2,1)S(1)} %copy-done.1, bf16[1024,13,128]{0,2,1:T(8,128)(2,1)} %bitcast.34, f32[128,13]{0,1:T(8,128)S(1)} %maximum_bitcast_fusion), kind=kOutput, calls=%fused_computation.18 | convolution fusion | flops 1339719680 | bytes 20879872 | tf_op jit(solution)/shard_map/hrk,khd->rhd/dot_general | solution.py:44
  264.6 1.4 copy.46
  266.0 1.1 convert_element_type.18
  267.3 32.2 %all-gather.5.cloned.1.call-done = bf16[256,6656]{1,0:T(8,128)(2,1)} async-done(((bf16[32,6656]{1,0:T(8,128)(2,1)}), bf16[256,6656]{1,0:T(8,128)(2,1)}) %all-gather.5.cloned.1.call-update) | async-done | bytes 3407888 | tf_op jit(solution)/shard_map/all_gather | solution.py:86
  299.5 5.5 %fusion.26 = (f32[256]{0:T(256)S(1)}, f32[256]{0:T(256)S(1)}, f32[256,384]{1,0:T(8,128)S(1)}) fusion(bf16[256,6656]{1,0:T(8,128)(2,1)} %all-gather.5.cloned.1.call-done, bf16[6656,384]{1,0:T(8,128)(2,1)} %param.9), kind=kOutput, calls=%fused_computation.39 | convolution fusion | flops 1308917248 | bytes 8914944 | tf_op jit(solution)/shard_map/dot_general | solution.py:85
  305.2 76.2 %all-reduce = (f32[32]{0:T(128)S(1)}, f32[32]{0:T(128)S(1)}) all-reduce(f32[32]{0:T(128)S(1)} %get-tuple-element.7, f32[32]{0:T(128)S(1)} %broadcast_multiply_fusion), channel_id=1, replica_groups=mesh['blk'=32,'tp'=8] {'blk','tp'}, use_global_device_ids=true, to_apply=%region_4.5 | all-reduce | flops 64 | bytes 512 | tf_op jit(solution)/shard_map/psum | solution.py:96
  381.5 74.0 %pmax.7 = f32[32]{0:T(128)S(1)} all-reduce(f32[32]{0:T(128)S(1)} %get-tuple-element.4), channel_id=1, replica_groups=mesh['blk'=32,'tp'=8] {'blk','tp'}, use_global_device_ids=true, to_apply=%region_10.11 | all-reduce | flops 32 | bytes 256 | tf_op jit(solution)/shard_map/pmax | solution.py:97
  455.5 0.5 mul.57
  456.0 0.8 multiply_convert_fusion
  (16 shorter events, 0.6 us)
Async XLA Ops:
  7.2 74.3 %all-gather.3.cloned.1.call-start = ((), (), s32[]{:S(2)}) async-start(), calls=%async_computation.1 | async-start | bytes 3833856 | tf_op jit(solution)/shard_map/all_gather | solution.py:60
  9.2 290.3 %all-gather.5.cloned.1.call-start = ((), (), s32[]{:S(2)}) async-start(), calls=%async_computation.2 | async-start | bytes 3833856 | tf_op jit(solution)/shard_map/all_gather | solution.py:86
  74.9 75.7 %collective-permute-start = (bf16[1024,1664]{1,0:T(8,128)(2,1)}, bf16[1024,1664]{1,0:T(8,128)(2,1)}, u32[]{:S(2)}, u32[]{:S(2)}) collective-permute-start(bf16[1024,1664]{1,0:T(8,128)(2,1)} %bitcast.32), channel_id=1, source_target_pairs={{0,8},{8,16},{16,24},{24,32},{32,40},{40,48},{48,56},{56,64},{64,7... | collective-permute-start | bytes 10223624 | tf_op jit(solution)/shard_map/ppermute | solution.py:29
  80.1 76.1 %collective-permute-start.1 = (bf16[1024,1664]{1,0:T(8,128)(2,1)}, bf16[1024,1664]{1,0:T(8,128)(2,1)}, u32[]{:S(2)}, u32[]{:S(2)}) collective-permute-start(bf16[1024,1664]{1,0:T(8,128)(2,1)} %bitcast.33), channel_id=1, source_target_pairs={{8,0},{16,8},{24,16},{32,24},{40,32},{48,40},{56,48},{64,56},{72,6... | collective-permute-start | bytes 10223624 | tf_op jit(solution)/shard_map/ppermute | solution.py:29
  81.4 142.3 %collective-permute-start.2 = (bf16[1024,1664]{0,1:T(8,128)(2,1)}, bf16[1024,1664]{0,1:T(8,128)(2,1)}, u32[]{:S(2)}, u32[]{:S(2)}) collective-permute-start(bf16[1024,1664]{0,1:T(8,128)(2,1)} %all-gather.3.cloned.1.call-done), channel_id=1, source_target_pairs={{0,8},{8,16},{16,24},{24,32},{32,40},{40,48},{48,56},{56,64},{64,7... | collective-permute-start | bytes 10223624 | tf_op jit(solution)/shard_map/ppermute | solution.py:29
  87.2 142.0 %collective-permute-start.3 = (bf16[1024,1664]{0,1:T(8,128)(2,1)}, bf16[1024,1664]{0,1:T(8,128)(2,1)}, u32[]{:S(2)}, u32[]{:S(2)}) collective-permute-start(bf16[1024,1664]{0,1:T(8,128)(2,1)} %all-gather.3.cloned.1.call-done), channel_id=1, source_target_pairs={{8,0},{16,8},{24,16},{32,24},{40,32},{48,40},{56,48},{64,56},{72,6... | collective-permute-start | bytes 10223624 | tf_op jit(solution)/shard_map/ppermute | solution.py:29
  104.5 124.8 %copy-start = (bf16[1024,1664]{0,1:T(8,128)(2,1)S(1)}, bf16[1024,1664]{0,1:T(8,128)(2,1)}, u32[]{:S(2)}) copy-start(bf16[1024,1664]{0,1:T(8,128)(2,1)} %all-gather.3.cloned.1.call-done) | copy-start | bytes 10223620
  237.2 18.0 %copy-start.1 = (bf16[1024,13,128]{0,2,1:T(8,128)(2,1)S(1)}, bf16[1024,13,128]{0,2,1:T(8,128)(2,1)}, u32[]{:S(2)}) copy-start(bf16[1024,13,128]{0,2,1:T(8,128)(2,1)} %concatenate.17) | copy-start | bytes 10223620
Sparse Core Ops, SparseCore 0:
  9.8 62.1 all-gather.2
  267.2 32.2 all-gather.4
